TPU v7x, 256 devices: a whole 4x4x8 slice. The times are simulated.
256 devices in a mesh: seq: 32 (over x, z_lo, core), mp: 8 (over y, z_hi).
Axes of the slice: x: 4, y: 4, z: 8 (z_hi: 2, z_lo: 4; z = z_hi * 4 + z_lo), core: 2. Of those that a mesh axis runs over, the one named last changes fastest.
Arguments:
- tokens: bfloat16 [8192, 4096], P('seq', 'mp'), may hold values from -6 to 6
- norm_gain: bfloat16 [4096], replicated, may hold values from 0.5 to 1.5
- norm_bias: bfloat16 [4096], replicated, may hold values from -4 to 4
- w_query: bfloat16 [4096, 2048], P(None, 'mp'), may hold values from -0.25 to 0.25
- w_keyval: bfloat16 [4096, 2, 2048], P(None, None, 'mp'), may hold values from -0.09375 to 0.09375
- w_out: bfloat16 [2048, 4096], P('mp'), may hold values from -0.125 to 0.125
- prefix_key: bfloat16 [8192, 2048], P('seq', 'mp'), may hold values from -82 to 82
- prefix_value: bfloat16 [8192, 2048], P('seq', 'mp'), may hold values from -6 to 6
- lengths: int32 [16], replicated, may hold values from 1 to 1024, 8192 in all
- context: int32 [16], replicated, may hold values from 256 to 8192
- prefix_place: int32 [64], replicated, may hold values from 0 to 63, each once
Outputs:
- attn_out: bfloat16 [8192, 4096], P(('seq', 'mp'))
Inputs may be any that keep to these rules, and one draw needn't show every extreme that they name: The lengths add up to 8192, and one request has exactly 1024 tokens. Stored block j holds the prefix positions prefix_place[j] * 128 to prefix_place[j] * 128 + 127; every block appears once.
All inputs are finite; a program needn't handle non-finite values.
Results may differ from a plain program's by a relative error of at most 0.02.
The roundings to bfloat16 on the way count: a program that leaves them out, or rounds other values in their place, can miss the bound.
Values may be sent and summed in bfloat16 or wider, within the bound.
No kernel may reach another device: no remote copies, remote signals or barrier semaphores. Data moves between devices by JAX's collectives and lax.ppermute only.
A program may use at most 128 MiB of HBM per device.

v0:
```python
import math
import jax
import jax.numpy as jnp
from jax import lax
from jax.sharding import PartitionSpec as P

HD = 128
PBLOCK = 128
NEG_FILL = -1e30


def layer_norm(rows_in, norm_gain, norm_bias):
    as_float = rows_in.astype(jnp.float32)
    row_mean = jnp.mean(as_float, -1, keepdims=True)
    centered = as_float - row_mean
    row_var = jnp.mean(centered * centered, -1, keepdims=True)
    scaled = centered * lax.rsqrt(row_var + 1e-05)
    return (scaled * norm_gain.astype(jnp.float32) + norm_bias.astype(jnp.float32)).astype(
        jnp.bfloat16
    )


def rotate(column_block, position):
    head_dim = column_block.shape[-1]
    half_rot = head_dim // 8
    inverse_freq = jnp.power(
        jnp.float32(10000.0), -jnp.arange(half_rot, dtype=jnp.float32) * (8.0 / head_dim)
    )
    angles = position.astype(jnp.float32)[:, None] * inverse_freq[None, :]
    cosine = jnp.cos(angles)[:, None, :]
    sines = jnp.sin(angles)[:, None, :]
    first_half = column_block[..., :half_rot]
    second = column_block[..., half_rot : 2 * half_rot]
    return jnp.concatenate(
        [
            first_half * cosine - second * sines,
            second * cosine + first_half * sines,
            column_block[..., 2 * half_rot :],
        ],
        -1,
    )


def request_info(global_index, lengths, context):
    request_end = jnp.cumsum(lengths)
    starts = request_end - lengths
    inside = (
        (global_index[:, None] >= starts[None, :]) & (global_index[:, None] < request_end[None, :])
    ).astype(jnp.int32)
    labels = jnp.arange(lengths.shape[0], dtype=jnp.int32) + 1
    request = jnp.sum(inside * labels[None, :], 1) - 1
    cached_len = jnp.sum(inside * context[None, :], 1)
    position = jnp.sum(inside * (context - starts)[None, :], 1) + global_index
    return (request, cached_len, position)


def masked_softmax_attention(queries, key_sets, value_sets, visible_sets):
    scale = 1.0 / math.sqrt(queries.shape[-1])
    score_sets = [
        jnp.einsum("qhd,khd->hqk", queries, keys, preferred_element_type=jnp.float32) * scale
        for keys in key_sets
    ]
    row_max = None
    for scores, visible in zip(score_sets, visible_sets):
        part = jnp.max(jnp.where(visible[None], scores, NEG_FILL), -1)
        row_max = part if row_max is None else jnp.maximum(row_max, part)
    row_sum = 0.0
    weighted = 0.0
    for scores, visible, values in zip(score_sets, visible_sets, value_sets):
        probs = jnp.where(visible[None], jnp.exp(scores - row_max[..., None]), 0.0)
        row_sum = row_sum + jnp.sum(probs, -1)
        weighted = weighted + jnp.einsum(
            "hqk,khd->hqd", probs.astype(jnp.bfloat16), values, preferred_element_type=jnp.float32
        )
    return weighted / row_sum[..., None]


SUFFIX_SHARDS = 5


def body(
    tokens,
    norm_gain,
    norm_bias,
    w_query,
    w_keyval,
    w_out,
    prefix_key,
    prefix_value,
    lengths,
    context,
    prefix_place,
):
    prefix_rows = prefix_key.shape[0]
    local_heads = w_query.shape[1] // HD
    prefix_both = lax.all_gather(
        jnp.stack([prefix_key, prefix_value], 0), "seq", axis=1, tiled=True
    )
    gathered = lax.all_gather(tokens, "mp", axis=1, tiled=True)
    token_count = gathered.shape[0]
    feature_count = gathered.shape[1]
    normed = layer_norm(gathered, norm_gain, norm_bias)
    seq_index = lax.axis_index("seq")
    seq_count = lax.psum(1, "seq")
    global_index = seq_index * token_count + jnp.arange(token_count, dtype=jnp.int32)
    request, cached_len, position = request_info(global_index, lengths, context)
    query_raw = jnp.dot(normed, w_query, preferred_element_type=jnp.float32).reshape(
        token_count, local_heads, HD
    )
    key_value_raw = jnp.dot(
        normed, w_keyval.reshape(feature_count, -1), preferred_element_type=jnp.float32
    ).reshape(token_count, 2, local_heads, HD)
    queries = rotate(query_raw, position).astype(jnp.bfloat16)
    own_keys = rotate(key_value_raw[:, 0], position).astype(jnp.bfloat16)
    own_values = key_value_raw[:, 1].astype(jnp.bfloat16)
    key_value = jnp.stack([own_keys, own_values], 0)
    window = [key_value]
    for shift in range(1, SUFFIX_SHARDS):
        pairs = [(i, i + shift) for i in range(seq_count - shift)]
        window.insert(0, lax.ppermute(key_value, "seq", pairs))
    window = jnp.concatenate(window, 1)
    window_count = window.shape[1]
    key_index = (seq_index - (SUFFIX_SHARDS - 1)) * token_count + jnp.arange(
        window_count, dtype=jnp.int32
    )
    key_request = request_info(key_index, lengths, context)[0]
    sees_suffix = (
        (key_index[None, :] >= 0)
        & (key_request[None, :] == request[:, None])
        & (key_index[None, :] <= global_index[:, None])
    )
    prefix_all = prefix_both.shape[1]
    prefix_position = (
        prefix_place[:, None] * PBLOCK + jnp.arange(PBLOCK, dtype=jnp.int32)[None, :]
    ).reshape(-1)
    sees_prefix = prefix_position[None, :] < cached_len[:, None]
    prefix_keys = prefix_both[0].reshape(prefix_all, local_heads, HD)
    prefix_values = prefix_both[1].reshape(prefix_all, local_heads, HD)
    attended = masked_softmax_attention(
        queries, (prefix_keys, window[0]), (prefix_values, window[1]), (sees_prefix, sees_suffix)
    )
    heads_out = (
        attended.astype(jnp.bfloat16).transpose(1, 0, 2).reshape(token_count, local_heads * HD)
    )
    summed = lax.psum_scatter(
        jnp.dot(heads_out, w_out, preferred_element_type=jnp.float32).astype(jnp.bfloat16),
        "mp",
        scatter_dimension=0,
        tiled=True,
    )
    return summed


def solution(mesh):
    return jax.shard_map(
        body,
        mesh=mesh,
        in_specs=(
            P("seq", "mp"),
            P(),
            P(),
            P(None, "mp"),
            P(None, None, "mp"),
            P("mp", None),
            P("seq", "mp"),
            P("seq", "mp"),
            P(),
            P(),
            P(),
        ),
        out_specs=P(("seq", "mp"), None),
        check_vma=False,
    )
```

profile of v0, /device:TPU:2, one launch (start us, length us, event | category | flops | bytes accessed | tf_op | source)
XLA Modules:
  0.0 328.7 jit_solution(272534547121617955)
XLA Ops:
  7.3 1.0 copy.50
  8.3 1.0 copy.49
  12.4 4.9 %copy.63 = bf16[512,8,2,256]{3,1,2,0:T(8,128)(2,1)} copy(bf16[512,8,2,256]{3,2,1,0:T(2,128)(2,1)} %bitcast.52) | data formatting | bytes 8388608
  17.3 6.4 %copy.52 = bf16[512,4096]{1,0:T(8,128)(2,1)} copy(bf16[512,4096]{0,1:T(8,128)(2,1)} %bitcast.51) | data formatting | bytes 8388608 | tf_op jit(solution)/shard_map/dot_general | solution.py:110
  24.5 2.6 broadcast_compare_fusion
  27.1 61.3 %all-gather.3.cloned.1.call-done = bf16[256,4096]{1,0:T(8,128)(2,1)} async-done(((bf16[256,512]{1,0:T(8,128)(2,1)}), bf16[256,4096]{1,0:T(8,128)(2,1)}) %all-gather.3.cloned.1.call-update) | async-done | bytes 2097168 | tf_op jit(solution)/shard_map/all_gather | solution.py:99
  88.4 2.1 convert_reduce_fusion
  90.5 2.3 fusion.7
  92.8 1.4 fusion.41
  94.5 4.1 %fusion.13 = f32[256,2,2,128]{3,0,2,1:T(8,128)S(1)} fusion(bf16[2,2,128,4096]{3,2,1,0:T(8,128)(2,1)} %bitcast.53, bf16[256,4096]{1,0:T(8,128)(2,1)} %all-gather.3.cloned.1.call-done, f32[4096]{0:T(1024)S(1)} %convert_element_type.57, f32[4096]{0:T(1024)S(1)} %convert_element_type.56, f32[256]{0:T(256)S(1)} %add_rsqrt_fusion, f32[256]{0:T(256)S(1)} %broadcast_multiply_fusion), kind=kOutput, calls=%fused_computation.21 | convolution fusion | flops 1080033280 | bytes 6850560 | tf_op jit(solution)/shard_map/dot_general | solution.py:110
  98.8 0.9 fusion.32
  99.9 2.8 collective-permute-start
  102.7 1.9 collective-permute-start.1
  104.6 3.6 %collective-permute-start.2 = (bf16[2,256,2,128]{3,1,2,0:T(8,128)(2,1)S(1)}, bf16[2,256,2,128]{3,1,2,0:T(8,128)(2,1)}, u32[]{:S(2)}, u32[]{:S(2)}) collective-permute-start(bf16[2,256,2,128]{3,1,2,0:T(8,128)(2,1)S(1)} %pad_maximum_fusion.1), channel_id=1, source_target_pairs={{0,16},{8,24},{16,32},{24,40},{32,48},{40,56},{48,64},{56,72},{64,... | collective-permute-start | bytes 786440 | tf_op jit(solution)/shard_map/ppermute | solution.py:120
  108.7 0.9 slice.53
  109.6 4.3 %collective-permute-start.3 = (bf16[2,256,2,128]{3,1,2,0:T(8,128)(2,1)S(1)}, bf16[2,256,2,128]{3,1,2,0:T(8,128)(2,1)}, u32[]{:S(2)}, u32[]{:S(2)}) collective-permute-start(bf16[2,256,2,128]{3,1,2,0:T(8,128)(2,1)S(1)} %pad_maximum_fusion.1), channel_id=1, source_target_pairs={{0,8},{8,16},{16,24},{24,32},{32,40},{40,48},{48,56},{56,64},{64,7... | collective-permute-start | bytes 786440 | tf_op jit(solution)/shard_map/ppermute | solution.py:120
  114.6 22.2 %collective-permute-done = bf16[2,256,2,128]{3,1,2,0:T(8,128)(2,1)} collective-permute-done((bf16[2,256,2,128]{3,1,2,0:T(8,128)(2,1)S(1)}, bf16[2,256,2,128]{3,1,2,0:T(8,128)(2,1)}, u32[]{:S(2)}, u32[]{:S(2)}) %collective-permute-start) | collective-permute-done | bytes 262176 | tf_op jit(solution)/shard_map/ppermute | solution.py:120
  136.8 1.0 constant_dynamic-update-slice_fusion.4
  137.8 2.9 collective-permute-done.1
  140.7 1.0 constant_dynamic-update-slice_fusion.3
  141.7 1.0 constant_dynamic-update-slice_fusion.2
  142.7 1.0 constant_dynamic-update-slice_fusion.1
  143.9 1.0 copy-done.9
  145.0 3.3 select_reduce_fusion.1
  148.3 45.9 %all-gather.5.cloned.1.call-done = bf16[2,8192,256]{1,2,0:T(8,128)(2,1)} async-done(((bf16[2,256,256]{1,2,0:T(8,128)(2,1)}), bf16[2,8192,256]{1,2,0:T(8,128)(2,1)}) %all-gather.5.cloned.1.call-update) | async-done | bytes 8388624 | tf_op jit(solution)/shard_map/all_gather | solution.py:96
  194.1 6.0 %fusion.44 = (bf16[1,8192,256]{1,2,0:T(8,128)(2,1)}, bf16[1,8192,256]{1,2,0:T(8,128)(2,1)}) fusion(bf16[2,8192,256]{1,2,0:T(8,128)(2,1)} %all-gather.5.cloned.1.call-done), kind=kLoop, calls=%fused_computation.79 | loop fusion | bytes 16777216 | tf_op jit(solution)/shard_map/slice | solution.py:137
  200.2 6.4 %select_reduce_fusion = (f32[2,256]{1,0:T(2,128)S(1)}, f32[2,256,8192]{2,1,0:T(8,128)S(1)}) fusion(pred[256,8192]{1,0:T(8,128)(4,1)S(1)} %copy-done.2, bf16[8192,2,128]{0,2,1:T(8,128)(2,1)} %bitcast.55, bf16[256,2,96]{2,0,1:T(8,128)(2,1)S(1)} %copy-done.7, bf16[256,2,16]{2,0,1:T(8,128)(2,1)S(1)} %copy-done.5, bf16[256,2,16]{2,0,1:T(8,128)(2,1)S(1)} %copy-done.6), kind=kOutput, calls=%fused_computation.1 | convolution fusion | flops 1086717440 | bytes 23201792 | tf_op jit(solution)/shard_map/qhd,khd->hqk/dot_general | solution.py:60
  206.7 4.8 %fusion = f32[2,256]{1,0:T(2,128)S(1)} fusion(f32[2,256,8192]{2,1,0:T(8,128)S(1)} %get-tuple-element.23, f32[2,256]{1,0:T(2,128)S(1)} %max.7, pred[256,8192]{1,0:T(8,128)(4,1)S(1)} %copy-done.2), kind=kLoop, calls=%fused_computation.2 | loop fusion | flops 16776704 | bytes 18878464 | tf_op jit(solution)/shard_map/reduce_sum | solution.py:71
  211.4 0.9 copy-done.1
  212.4 9.4 %fusion.2 = f32[2,256,128]{1,2,0:T(8,128)S(1)} fusion(bf16[8192,2,128]{0,2,1:T(8,128)(2,1)} %bitcast.54, f32[2,256,8192]{2,1,0:T(8,128)} %copy-done.1, f32[2,256]{1,0:T(2,128)S(1)} %max.7, pred[256,8192]{1,0:T(8,128)(4,1)S(1)} %copy-done.2), kind=kOutput, calls=%fused_computation.4 | convolution fusion | flops 1090519040 | bytes 23332864 | tf_op jit(solution)/shard_map/hqk,khd->hqd/dot_general | solution.py:72
  223.4 2.1 convolution_convert_fusion
  225.5 96.6 %reduce-scatter.2.cloned.1.call-done = bf16[32,4096]{1,0:T(8,128)(2,1)} async-done(((bf16[256,4096]{1,0:T(8,128)(2,1)}), bf16[32,4096]{1,0:T(8,128)(2,1)}) %reduce-scatter.2.cloned.1.call-update) | async-done | bytes 262160 | tf_op jit(solution)/shard_map/reduce_scatter | solution.py:145
  (73 shorter events, 8.0 us)
Async XLA Ops:
  6.5 216.9 %copy-start = (bf16[256,4096]{1,0:T(8,128)(2,1)S(1)}, bf16[256,4096]{1,0:T(8,128)(2,1)}, u32[]{:S(2)}) copy-start(bf16[256,4096]{1,0:T(8,128)(2,1)} %param.16) | copy-start | bytes 6291460
  6.5 81.9 %all-gather.3.cloned.1.call-start = ((), (), s32[]{:S(2)}) async-start(), calls=%async_computation.1 | async-start | bytes 2359296 | tf_op jit(solution)/shard_map/all_gather | solution.py:99
  7.3 186.9 %all-gather.5.cloned.1.call-start = ((), (), s32[]{:S(2)}) async-start(), calls=%async_computation.2 | async-start | bytes 8650752 | tf_op jit(solution)/shard_map/all_gather | solution.py:96
  10.1 312.1 %reduce-scatter.2.cloned.1.call-start = ((), (), s32[]{:S(2)}) async-start(), calls=%async_computation.3 | async-start | bytes 2359296 | tf_op jit(solution)/shard_map/reduce_scatter | solution.py:145
  17.3 6.5 %copy-start.11 = (s32[16]{0:T(128)S(1)}, s32[16]{0:T(128)}, u32[]{:S(2)}) copy-start(s32[16]{0:T(128)} %param.19) | copy-start | bytes 196
  17.3 6.5 %copy-start.12 = (s32[16]{0:T(128)S(1)}, s32[16]{0:T(128)}, u32[]{:S(2)}) copy-start(s32[16]{0:T(128)} %param.20) | copy-start | bytes 196
  17.3 7.1 %copy-start.14 = (s32[64]{0:T(128)S(1)}, s32[64]{0:T(128)}, u32[]{:S(2)}) copy-start(s32[64]{0:T(128)} %param.21) | copy-start | bytes 772
  88.4 4.4 %copy-start.3 = (bf16[256,4096]{1,0:T(8,128)(2,1)S(1)}, bf16[256,4096]{1,0:T(8,128)(2,1)}, u32[]{:S(2)}) copy-start(bf16[256,4096]{1,0:T(8,128)(2,1)} %all-gather.3.cloned.1.call-done) | copy-start | bytes 6291460
  88.4 4.4 %copy-start.13 = (bf16[4096,256]{1,0:T(8,128)(2,1)S(1)}, bf16[4096,256]{1,0:T(8,128)(2,1)}, u32[]{:S(2)}) copy-start(bf16[4096,256]{1,0:T(8,128)(2,1)} %param.14) | copy-start | bytes 6291460
  94.3 4.4 %copy-start.8 = (f32[256,256]{0,1:T(8,128)}, f32[256,256]{0,1:T(8,128)S(1)}, u32[]{:S(2)}) copy-start(f32[256,256]{0,1:T(8,128)S(1)} %fusion.41) | copy-start | bytes 786436
  99.7 45.2 %copy-start.5 = (bf16[256,2,16]{2,0,1:T(8,128)(2,1)S(1)}, bf16[256,2,16]{2,0,1:T(8,128)(2,1)}, u32[]{:S(2)}) copy-start(bf16[256,2,16]{2,0,1:T(8,128)(2,1)} %get-tuple-element.16) | copy-start | bytes 49156
  99.9 36.9 %collective-permute-start = (bf16[2,256,2,128]{3,1,2,0:T(8,128)(2,1)S(1)}, bf16[2,256,2,128]{3,1,2,0:T(8,128)(2,1)}, u32[]{:S(2)}, u32[]{:S(2)}) collective-permute-start(bf16[2,256,2,128]{3,1,2,0:T(8,128)(2,1)S(1)} %pad_maximum_fusion.1), channel_id=1, source_target_pairs={{0,32},{8,40},{16,48},{24,56},{32,64},{40,72},{48,80},{56,88},{64,... | collective-permute-start | bytes 786440 | tf_op jit(solution)/shard_map/ppermute | solution.py:120
  102.7 38.0 %collective-permute-start.1 = (bf16[2,256,2,128]{3,1,2,0:T(8,128)(2,1)S(1)}, bf16[2,256,2,128]{3,1,2,0:T(8,128)(2,1)}, u32[]{:S(2)}, u32[]{:S(2)}) collective-permute-start(bf16[2,256,2,128]{3,1,2,0:T(8,128)(2,1)S(1)} %pad_maximum_fusion.1), channel_id=1, source_target_pairs={{0,24},{8,32},{16,40},{24,48},{32,56},{40,64},{48,72},{56,80},{64,... | collective-permute-start | bytes 786440 | tf_op jit(solution)/shard_map/ppermute | solution.py:120
  104.6 37.1 %collective-permute-start.2 = (bf16[2,256,2,128]{3,1,2,0:T(8,128)(2,1)S(1)}, bf16[2,256,2,128]{3,1,2,0:T(8,128)(2,1)}, u32[]{:S(2)}, u32[]{:S(2)}) collective-permute-start(bf16[2,256,2,128]{3,1,2,0:T(8,128)(2,1)S(1)} %pad_maximum_fusion.1), channel_id=1, source_target_pairs={{0,16},{8,24},{16,32},{24,40},{32,48},{40,56},{48,64},{56,72},{64,... | collective-permute-start | bytes 786440 | tf_op jit(solution)/shard_map/ppermute | solution.py:120
  109.6 33.1 %collective-permute-start.3 = (bf16[2,256,2,128]{3,1,2,0:T(8,128)(2,1)S(1)}, bf16[2,256,2,128]{3,1,2,0:T(8,128)(2,1)}, u32[]{:S(2)}, u32[]{:S(2)}) collective-permute-start(bf16[2,256,2,128]{3,1,2,0:T(8,128)(2,1)S(1)} %pad_maximum_fusion.1), channel_id=1, source_target_pairs={{0,8},{8,16},{16,24},{24,32},{32,40},{40,48},{48,56},{56,64},{64,7... | collective-permute-start | bytes 786440 | tf_op jit(solution)/shard_map/ppermute | solution.py:120
  143.9 1.1 copy-start.9
  148.3 51.9 %copy-start.6 = (bf16[256,2,16]{2,0,1:T(8,128)(2,1)S(1)}, bf16[256,2,16]{2,0,1:T(8,128)(2,1)}, u32[]{:S(2)}) copy-start(bf16[256,2,16]{2,0,1:T(8,128)(2,1)} %get-tuple-element.17) | copy-start | bytes 49156
  148.3 51.9 %copy-start.7 = (bf16[256,2,96]{2,0,1:T(8,128)(2,1)S(1)}, bf16[256,2,96]{2,0,1:T(8,128)(2,1)}, u32[]{:S(2)}) copy-start(bf16[256,2,96]{2,0,1:T(8,128)(2,1)} %copy.62) | copy-start | bytes 294916
  194.1 6.0 %copy-start.2 = (pred[256,8192]{1,0:T(8,128)(4,1)S(1)}, pred[256,8192]{1,0:T(8,128)(4,1)}, u32[]{:S(2)}) copy-start(pred[256,8192]{1,0:T(8,128)(4,1)} %broadcast_compare_fusion) | copy-start | bytes 6291460
  206.6 5.7 %copy-start.1 = (f32[2,256,8192]{2,1,0:T(8,128)}, f32[2,256,8192]{2,1,0:T(8,128)S(1)}, u32[]{:S(2)}) copy-start(f32[2,256,8192]{2,1,0:T(8,128)S(1)} %get-tuple-element.23) | copy-start | bytes 50331652
  212.3 9.5 %copy-start.4 = (f32[2,256,1280]{2,1,0:T(8,128)S(1)}, f32[2,256,1280]{2,1,0:T(8,128)}, u32[]{:S(2)}) copy-start(f32[2,256,1280]{2,1,0:T(8,128)} %get-tuple-element.25) | copy-start | bytes 7864324
  212.3 10.3 %copy-start.10 = (bf16[2,1280,2,128]{3,1,2,0:T(8,128)(2,1)S(1)}, bf16[2,1280,2,128]{3,1,2,0:T(8,128)(2,1)}, u32[]{:S(2)}) copy-start(bf16[2,1280,2,128]{3,1,2,0:T(8,128)(2,1)} %copy-done.9) | copy-start | bytes 3932164
Sparse Core Ops, SparseCore 0:
  9.8 78.5 all-gather.2
  90.2 103.9 all-gather.4
  225.7 96.4 reduce-scatter.1
where the time goes:
time: 329 us
  waiting for transfers between devices  230 us (70%)
  local copies, waits for them, and re-layouts  28.3 us (9%)
  matrix products  27.6 us (8%)
  other arithmetic  17 us (5%)
  between operations  13.5 us (4%)
  starting transfers between devices  12.7 us (4%)
    reduce_scatter x1, waiting for transfers between devices, body(): lax.psum_scatter(jnp.dot(heads_out, w_out, preferred_element_type=jnp.flo...  96.6 us
    all_gather x1, waiting for transfers between devices, body(): gathered = lax.all_gather(tokens, 'mp', axis=1, tiled=True)  61.3 us
    all_gather x1, waiting for transfers between devices, body(): lax.all_gather(jnp.stack([prefix_key, prefix_value], 0), 'seq', axis=1, t...  45.9 us
    ppermute x4, waiting for transfers between devices, body(): window.insert(0, lax.ppermute(key_value, 'seq', pairs))  25.1 us
    unnamed x40, local copies, waits for them, and re-layouts  13.8 us
    ppermute x4, starting transfers between devices, body(): window.insert(0, lax.ppermute(key_value, 'seq', pairs))  12.6 us
    dot_general x2, matrix products, masked_softmax_attention(): jnp.einsum('hqk,khd->hqd', probs.astype(jnp.bfloat16), values, preferred_...  10.2 us
    dot_general x2, matrix products, masked_softmax_attention(): jnp.einsum('qhd,khd->hqk', queries, keys, preferred_element_type=jnp.floa...  9.72 us
  transfers between devices with their start and end apart: 7, of which 5 were waited for; matrix products, arithmetic and copies ran while one was open for 12% of the time, Pallas kernels for 0%

commit v1 on v0

--- a/solution.py
+++ b/solution.py
@@ -96,7 +96,9 @@
     prefix_both = lax.all_gather(
         jnp.stack([prefix_key, prefix_value], 0), "seq", axis=1, tiled=True
     )
-    gathered = lax.all_gather(tokens, "mp", axis=1, tiled=True)
+    gathered = jnp.concatenate(
+        lax.all_to_all(jnp.stack([tokens] * lax.axis_size("mp")), "mp", 0, 0), axis=1
+    )
     token_count = gathered.shape[0]
     feature_count = gathered.shape[1]
     normed = layer_norm(gathered, norm_gain, norm_bias)

time: 329 us -> 298 us (0.906)
  waiting for transfers between devices: 230 us -> 188 us
  starting transfers between devices: 12.7 us -> 24.3 us
  local copies, waits for them, and re-layouts: 28.3 us -> 34 us
  matrix products: 27.6 us -> 22.6 us
    all_gather x1 -> x0, waiting for transfers between devices: 61.3 us -> none  [body(): gathered = lax.all_gather(tokens, 'mp', axis=1, tiled=True)]
    all_to_all x0 -> x1, waiting for transfers between devices: none -> 33.8 us  [body(): lax.all_to_all(jnp.stack([tokens] * lax.axis_size('mp')), 'mp', 0, 0)]
    all_gather x1, waiting for transfers between devices: 45.9 us -> 12.5 us  [body(): lax.all_gather(jnp.stack([prefix_key, prefix_value], 0), 'seq', axis=1, t...]
    ppermute x4, waiting for transfers between devices: 25.1 us -> 44.3 us  [body(): window.insert(0, lax.ppermute(key_value, 'seq', pairs))]
    all_to_all x0 -> x1, starting transfers between devices: none -> 11.2 us  [body(): lax.all_to_all(jnp.stack([tokens] * lax.axis_size('mp')), 'mp', 0, 0)]
    dot_general x0 -> x1, local copies, waits for them, and re-layouts: none -> 4.21 us  [body(): jnp.dot(normed, w_query, preferred_element_type=jnp.float32)]
    all_to_all x0 -> x1, local copies, waits for them, and re-layouts: none -> 3.91 us  [body(): lax.all_to_all(jnp.stack([tokens] * lax.axis_size('mp')), 'mp', 0, 0)]
    unnamed x40 -> x35, local copies, waits for them, and re-layouts: 13.8 us -> 10.8 us
where the time goes in v1:
time: 298 us; the launch traced here: 297 us
  waiting for transfers between devices  188 us (63%)
  local copies, waits for them, and re-layouts  34 us (11%)
  starting transfers between devices  24.3 us (8%)
  matrix products  22.6 us (8%)
  other arithmetic  14.3 us (5%)
  between operations  13.8 us (5%)
    reduce_scatter x1, waiting for transfers between devices, body(): lax.psum_scatter(jnp.dot(heads_out, w_out, preferred_element_type=jnp.flo...  97.5 us
    ppermute x4, waiting for transfers between devices, body(): window.insert(0, lax.ppermute(key_value, 'seq', pairs))  44.3 us
    all_to_all x1, waiting for transfers between devices, body(): lax.all_to_all(jnp.stack([tokens] * lax.axis_size('mp')), 'mp', 0, 0)  33.8 us
    ppermute x4, starting transfers between devices, body(): window.insert(0, lax.ppermute(key_value, 'seq', pairs))  13.1 us
    all_gather x1, waiting for transfers between devices, body(): lax.all_gather(jnp.stack([prefix_key, prefix_value], 0), 'seq', axis=1, t...  12.5 us
    all_to_all x1, starting transfers between devices, body(): lax.all_to_all(jnp.stack([tokens] * lax.axis_size('mp')), 'mp', 0, 0)  11.2 us
    unnamed x35, local copies, waits for them, and re-layouts  10.8 us
    dot_general x2, matrix products, masked_softmax_attention(): jnp.einsum('hqk,khd->hqd', probs.astype(jnp.bfloat16), values, preferred_...  10.2 us
  transfers between devices with their start and end apart: 7, of which 5 were waited for; matrix products, arithmetic and copies ran while one was open for 12% of the time, Pallas kernels for 0%

profile of v1, /device:TPU:2, one launch (start us, length us, event | category | flops | bytes accessed | tf_op | source)
XLA Modules:
  0.0 297.1 jit_solution(17618882373564458748)
XLA Ops:
  6.5 1.1 copy.54
  7.7 1.0 copy.53
  8.7 0.7 pad_maximum_fusion
  9.5 2.5 stack.10
  11.9 11.2 %all-to-all-start = ((bf16[8,256,512]{2,1,0:T(8,128)(2,1)}), bf16[8,256,512]{2,1,0:T(8,128)(2,1)}, u32[]{:S(2)}, u32[]{:S(2)}) async-start(bf16[8,256,512]{2,1,0:T(8,128)(2,1)} %stack.10), calls=%async_computation | async-start | bytes 4194304 | tf_op jit(solution)/shard_map/all_to_all | solution.py:100
  23.6 4.2 %copy.68 = bf16[256,4096]{1,0:T(8,128)(2,1)} copy(bf16[256,4096]{0,1:T(8,128)(2,1)} %bitcast.64) | data formatting | bytes 4194304 | tf_op jit(solution)/shard_map/dot_general | solution.py:109
  27.8 4.9 %copy.70 = bf16[512,8,2,256]{3,1,2,0:T(8,128)(2,1)} copy(bf16[512,8,2,256]{3,2,1,0:T(2,128)(2,1)} %bitcast.60) | data formatting | bytes 8388608
  32.7 6.4 %copy.57 = bf16[512,4096]{1,0:T(8,128)(2,1)} copy(bf16[512,4096]{0,1:T(8,128)(2,1)} %bitcast.56) | data formatting | bytes 8388608 | tf_op jit(solution)/shard_map/dot_general | solution.py:112
  39.6 2.6 broadcast_compare_fusion
  42.2 33.8 %all-to-all-done = bf16[8,256,512]{2,1,0:T(8,128)(2,1)} async-done(((bf16[8,256,512]{2,1,0:T(8,128)(2,1)}), bf16[8,256,512]{2,1,0:T(8,128)(2,1)}, u32[]{:S(2)}, u32[]{:S(2)}) %all-to-all-start) | async-done | bytes 2097184 | tf_op jit(solution)/shard_map/all_to_all | solution.py:100
  76.0 3.9 %copy.50 = bf16[8,256,512]{1,2,0:T(8,128)(2,1)} copy(bf16[8,256,512]{2,1,0:T(8,128)(2,1)} %all-to-all-done) | data formatting | bytes 4194304 | tf_op jit(solution)/shard_map/all_to_all | solution.py:100
  80.0 2.3 convert_reduce_fusion
  82.9 1.4 fusion.10
  84.3 0.8 copy-done.5
  85.1 1.2 fusion.43
  87.5 4.0 %collective-permute-start = (bf16[2,256,2,128]{1,3,2,0:T(8,128)(2,1)S(1)}, bf16[2,256,2,128]{1,3,2,0:T(8,128)(2,1)S(1)}, u32[]{:S(2)}, u32[]{:S(2)}) collective-permute-start(bf16[2,256,2,128]{1,3,2,0:T(8,128)(2,1)S(1)} %pad_maximum_fusion.1), channel_id=1, source_target_pairs={{0,32},{8,40},{16,48},{24,56},{32,64},{40,72},{48,80},{56,88},{64,... | collective-permute-start | bytes 786440 | tf_op jit(solution)/shard_map/ppermute | solution.py:122
  91.5 1.9 collective-permute-start.1
  93.5 1.9 collective-permute-start.2
  95.8 5.2 %collective-permute-start.3 = (bf16[2,256,2,128]{1,3,2,0:T(8,128)(2,1)S(1)}, bf16[2,256,2,128]{1,3,2,0:T(8,128)(2,1)S(1)}, u32[]{:S(2)}, u32[]{:S(2)}) collective-permute-start(bf16[2,256,2,128]{1,3,2,0:T(8,128)(2,1)S(1)} %pad_maximum_fusion.1), channel_id=1, source_target_pairs={{0,8},{8,16},{16,24},{24,32},{32,40},{40,48},{48,56},{56,64},{64,7... | collective-permute-start | bytes 786440 | tf_op jit(solution)/shard_map/ppermute | solution.py:122
  101.0 27.7 %collective-permute-done = bf16[2,256,2,128]{1,3,2,0:T(8,128)(2,1)S(1)} collective-permute-done((bf16[2,256,2,128]{1,3,2,0:T(8,128)(2,1)S(1)}, bf16[2,256,2,128]{1,3,2,0:T(8,128)(2,1)S(1)}, u32[]{:S(2)}, u32[]{:S(2)}) %collective-permute-start) | collective-permute-done | bytes 262176 | tf_op jit(solution)/shard_map/ppermute | solution.py:122
  128.8 16.6 %collective-permute-done.1 = bf16[2,256,2,128]{1,3,2,0:T(8,128)(2,1)S(1)} collective-permute-done((bf16[2,256,2,128]{1,3,2,0:T(8,128)(2,1)S(1)}, bf16[2,256,2,128]{1,3,2,0:T(8,128)(2,1)S(1)}, u32[]{:S(2)}, u32[]{:S(2)}) %collective-permute-start.1) | collective-permute-done | bytes 262176 | tf_op jit(solution)/shard_map/ppermute | solution.py:122
  145.5 1.0 copy-done.7
  146.6 2.3 select_reduce_fusion.1
  148.9 12.5 %all-gather.2.cloned.1.call-done = bf16[2,8192,256]{1,2,0:T(8,128)(2,1)} async-done(((bf16[2,256,256]{1,2,0:T(8,128)(2,1)}), bf16[2,8192,256]{1,2,0:T(8,128)(2,1)}) %all-gather.2.cloned.1.call-update) | async-done | bytes 8388624 | tf_op jit(solution)/shard_map/all_gather | solution.py:96
  161.3 6.0 %fusion.41 = (bf16[1,8192,256]{1,2,0:T(8,128)(2,1)}, bf16[1,8192,256]{1,2,0:T(8,128)(2,1)}) fusion(bf16[2,8192,256]{1,2,0:T(8,128)(2,1)} %all-gather.2.cloned.1.call-done), kind=kLoop, calls=%fused_computation.79 | loop fusion | bytes 16777216 | tf_op jit(solution)/shard_map/slice | solution.py:139
  167.4 6.1 %select_reduce_fusion = (f32[2,256]{1,0:T(2,128)S(1)}, f32[2,256,8192]{2,1,0:T(8,128)S(1)}) fusion(pred[256,8192]{1,0:T(8,128)(4,1)S(1)} %copy-done.3, bf16[8192,2,128]{0,2,1:T(8,128)(2,1)} %bitcast.63, bf16[256,2,96]{0,2,1:T(8,128)(2,1)S(1)} %slice.91, bf16[256,2,16]{0,2,1:T(8,128)(2,1)S(1)} %get-tuple-element.16, bf16[256,2,16]{0,2,1:T(8,128)(2,1)S(1)} %get-tuple-element.17), kind=kOutput, calls=%fused_computation.1 | convolution fusion | flops 1086717440 | bytes 23201792 | tf_op jit(solution)/shard_map/qhd,khd->hqk/dot_general | solution.py:60
  173.5 4.8 %fusion = f32[2,256]{1,0:T(2,128)S(1)} fusion(f32[2,256,8192]{2,1,0:T(8,128)S(1)} %get-tuple-element.21, f32[2,256]{1,0:T(2,128)S(1)} %max.7, pred[256,8192]{1,0:T(8,128)(4,1)S(1)} %copy-done.3), kind=kLoop, calls=%fused_computation.2 | loop fusion | flops 16776704 | bytes 18878464 | tf_op jit(solution)/shard_map/reduce_sum | solution.py:71
  178.3 0.9 copy-done.2
  179.2 9.4 %fusion.2 = f32[2,256,128]{1,2,0:T(8,128)S(1)} fusion(bf16[8192,2,128]{0,2,1:T(8,128)(2,1)} %bitcast.62, f32[2,256,8192]{2,1,0:T(8,128)} %copy-done.2, f32[2,256]{1,0:T(2,128)S(1)} %max.7, pred[256,8192]{1,0:T(8,128)(4,1)S(1)} %copy-done.3), kind=kOutput, calls=%fused_computation.4 | convolution fusion | flops 1090519040 | bytes 23332864 | tf_op jit(solution)/shard_map/hqk,khd->hqd/dot_general | solution.py:72
  188.6 0.8 fusion.11
  190.7 2.1 convolution_convert_fusion
  192.8 97.5 %reduce-scatter.2.cloned.1.call-done = bf16[32,4096]{1,0:T(8,128)(2,1)} async-done(((bf16[256,4096]{1,0:T(8,128)(2,1)}), bf16[32,4096]{1,0:T(8,128)(2,1)}) %reduce-scatter.2.cloned.1.call-update) | async-done | bytes 262160 | tf_op jit(solution)/shard_map/reduce_scatter | solution.py:147
  (68 shorter events, 4.3 us)
Async XLA Ops:
  6.5 184.1 %copy-start = (bf16[256,4096]{1,0:T(8,128)(2,1)S(1)}, bf16[256,4096]{1,0:T(8,128)(2,1)}, u32[]{:S(2)}) copy-start(bf16[256,4096]{1,0:T(8,128)(2,1)} %param.16) | copy-start | bytes 6291460
  6.5 154.8 %all-gather.2.cloned.1.call-start = ((), (), s32[]{:S(2)}) async-start(), calls=%async_computation.2 | async-start | bytes 8650752 | tf_op jit(solution)/shard_map/all_gather | solution.py:96
  11.9 11.3 %copy-start.11 = (s32[16]{0:T(128)S(1)}, s32[16]{0:T(128)}, u32[]{:S(2)}) copy-start(s32[16]{0:T(128)} %param.19) | copy-start | bytes 196
  11.9 11.6 %copy-start.9 = (bf16[4096]{0:T(1024)(128)(2,1)S(1)}, bf16[4096]{0:T(1024)(128)(2,1)}, u32[]{:S(2)}) copy-start(bf16[4096]{0:T(1024)(128)(2,1)} %param.13) | copy-start | bytes 24580
  11.9 11.6 %copy-start.10 = (bf16[4096]{0:T(1024)(128)(2,1)S(1)}, bf16[4096]{0:T(1024)(128)(2,1)}, u32[]{:S(2)}) copy-start(bf16[4096]{0:T(1024)(128)(2,1)} %param.12) | copy-start | bytes 24580
  11.9 64.1 %all-to-all-start = ((bf16[8,256,512]{2,1,0:T(8,128)(2,1)}), bf16[8,256,512]{2,1,0:T(8,128)(2,1)}, u32[]{:S(2)}, u32[]{:S(2)}) async-start(bf16[8,256,512]{2,1,0:T(8,128)(2,1)} %stack.10), calls=%async_computation | async-start | bytes 4194304 | tf_op jit(solution)/shard_map/all_to_all | solution.py:100
  23.2 267.2 %reduce-scatter.2.cloned.1.call-start = ((), (), s32[]{:S(2)}) async-start(), calls=%async_computation.3 | async-start | bytes 2359296 | tf_op jit(solution)/shard_map/reduce_scatter | solution.py:147
  32.7 6.4 %copy-start.12 = (s32[16]{0:T(128)S(1)}, s32[16]{0:T(128)}, u32[]{:S(2)}) copy-start(s32[16]{0:T(128)} %param.20) | copy-start | bytes 196
  32.7 6.6 %copy-start.13 = (s32[64]{0:T(128)S(1)}, s32[64]{0:T(128)}, u32[]{:S(2)}) copy-start(s32[64]{0:T(128)} %param.21) | copy-start | bytes 772
  80.0 2.3 copy-start.1
  82.9 2.2 copy-start.5
  85.1 1.6 copy-start.4
  87.5 41.3 %collective-permute-start = (bf16[2,256,2,128]{1,3,2,0:T(8,128)(2,1)S(1)}, bf16[2,256,2,128]{1,3,2,0:T(8,128)(2,1)S(1)}, u32[]{:S(2)}, u32[]{:S(2)}) collective-permute-start(bf16[2,256,2,128]{1,3,2,0:T(8,128)(2,1)S(1)} %pad_maximum_fusion.1), channel_id=1, source_target_pairs={{0,32},{8,40},{16,48},{24,56},{32,64},{40,72},{48,80},{56,88},{64,... | collective-permute-start | bytes 786440 | tf_op jit(solution)/shard_map/ppermute | solution.py:122
  91.5 53.9 %collective-permute-start.1 = (bf16[2,256,2,128]{1,3,2,0:T(8,128)(2,1)S(1)}, bf16[2,256,2,128]{1,3,2,0:T(8,128)(2,1)S(1)}, u32[]{:S(2)}, u32[]{:S(2)}) collective-permute-start(bf16[2,256,2,128]{1,3,2,0:T(8,128)(2,1)S(1)} %pad_maximum_fusion.1), channel_id=1, source_target_pairs={{0,24},{8,32},{16,40},{24,48},{32,56},{40,64},{48,72},{56,80},{64,... | collective-permute-start | bytes 786440 | tf_op jit(solution)/shard_map/ppermute | solution.py:122
  93.5 52.0 %collective-permute-start.2 = (bf16[2,256,2,128]{1,3,2,0:T(8,128)(2,1)S(1)}, bf16[2,256,2,128]{1,3,2,0:T(8,128)(2,1)S(1)}, u32[]{:S(2)}, u32[]{:S(2)}) collective-permute-start(bf16[2,256,2,128]{1,3,2,0:T(8,128)(2,1)S(1)} %pad_maximum_fusion.1), channel_id=1, source_target_pairs={{0,16},{8,24},{16,32},{24,40},{32,48},{40,56},{48,64},{56,72},{64,... | collective-permute-start | bytes 786440 | tf_op jit(solution)/shard_map/ppermute | solution.py:122
  95.8 49.6 %collective-permute-start.3 = (bf16[2,256,2,128]{1,3,2,0:T(8,128)(2,1)S(1)}, bf16[2,256,2,128]{1,3,2,0:T(8,128)(2,1)S(1)}, u32[]{:S(2)}, u32[]{:S(2)}) collective-permute-start(bf16[2,256,2,128]{1,3,2,0:T(8,128)(2,1)S(1)} %pad_maximum_fusion.1), channel_id=1, source_target_pairs={{0,8},{8,16},{16,24},{24,32},{32,40},{40,48},{48,56},{56,64},{64,7... | collective-permute-start | bytes 786440 | tf_op jit(solution)/shard_map/ppermute | solution.py:122
  145.5 1.1 copy-start.7
  161.3 6.0 %copy-start.3 = (pred[256,8192]{1,0:T(8,128)(4,1)S(1)}, pred[256,8192]{1,0:T(8,128)(4,1)}, u32[]{:S(2)}) copy-start(pred[256,8192]{1,0:T(8,128)(4,1)} %broadcast_compare_fusion) | copy-start | bytes 6291460
  173.4 5.7 %copy-start.2 = (f32[2,256,8192]{2,1,0:T(8,128)}, f32[2,256,8192]{2,1,0:T(8,128)S(1)}, u32[]{:S(2)}) copy-start(f32[2,256,8192]{2,1,0:T(8,128)S(1)} %get-tuple-element.21) | copy-start | bytes 50331652
  179.2 9.5 %copy-start.6 = (f32[2,256,1280]{2,1,0:T(8,128)S(1)}, f32[2,256,1280]{2,1,0:T(8,128)}, u32[]{:S(2)}) copy-start(f32[2,256,1280]{2,1,0:T(8,128)} %get-tuple-element.23) | copy-start | bytes 7864324
  188.6 1.3 copy-start.8
Sparse Core Ops, SparseCore 0:
  9.6 151.6 all-gather.1
  192.9 97.3 reduce-scatter.1
